TPU v7x, 32 devices: a whole 2x2x4 slice. The times are simulated.
32 devices in a mesh: cuts: 2 (over x), mode: 16 (over z, y, core).
Axes of the slice: x: 2, y: 2, z: 4, core: 2. Of those that a mesh axis runs over, the one named last changes fastest.
Arguments:
- stem_blocks: bfloat16 [2, 4096, 2, 256], P('cuts', 'mode'), may hold values from -6 to 6
- w1_table: bfloat16 [8, 2, 256, 256], replicated, may hold values from -0.25 to 0.25
- w2_table: bfloat16 [8, 2, 256, 256], replicated, may hold values from -0.125 to 0.125
- slice_ids: int32 [2, 2, 2], P('cuts'), may hold values from 0 to 7, as said below
- mode_perm: int32 [256], replicated, may hold values from 0 to 255, each once
Outputs:
- amplitudes: float32 [256, 16, 2, 256], P('mode', 'cuts')
Inputs may be any that keep to these rules, and one draw needn't show every extreme that they name: For each stem block b, the 2 values slice_ids[:,b,0] are distinct, and so are the 2 values slice_ids[:,b,1]. `mode_perm`: each column appears once.
All inputs are finite; a program needn't handle non-finite values.
Results may differ from a plain program's by a relative error of at most 0.0029.
Values may be sent and summed in bfloat16 or wider, within the bound.
No kernel may reach another device: no remote copies, remote signals or barrier semaphores. Data moves between devices by JAX's collectives and lax.ppermute only.
A program may use at most 64 MiB of HBM per device.

v0:
```python
import jax
import jax.numpy as jnp
from jax import lax
from jax.sharding import PartitionSpec as P


def broadcast(block, axis, source):
    block = jnp.where(lax.axis_index(axis) == source, block, jnp.zeros_like(block))
    return lax.psum(block, axis)


def widen_first(entry):
    real_part, imag_part = (entry[0], entry[1])
    upper = jnp.concatenate([real_part, imag_part], axis=1)
    lower = jnp.concatenate([-imag_part, real_part], axis=1)
    return jnp.concatenate([upper, lower], axis=0)


def widen_second(entry):
    real_part, imag_part = (entry[0], entry[1])
    first_row = jnp.concatenate([real_part, imag_part], axis=1)
    second_row = jnp.concatenate([-imag_part, real_part], axis=1)
    return jnp.stack([first_row, second_row], axis=0)


def second_step(exchanged, weight_two, contract_cols, free_cols):
    block_count, mode_count, piece_rows, _ = exchanged.shape
    pieces = exchanged.reshape(block_count, mode_count, piece_rows, 2, contract_cols, free_cols)
    wide_out = weight_two.shape[3]
    shaped = weight_two.reshape(block_count, 2, mode_count, contract_cols, wide_out)
    return jnp.einsum("nhqpcs,nphco->qso", pieces, shaped, preferred_element_type=jnp.float32)


def on_device(stem_blocks, w1_table, w2_table, slice_ids, mode_perm):
    mode_count = lax.axis_size("mode")
    row_count = stem_blocks.shape[1]
    stem_width = stem_blocks.shape[3]
    mid_width = w1_table.shape[3]
    inner_width = w2_table.shape[2]
    out_width = w2_table.shape[3]
    piece_rows = row_count // mode_count
    contract_cols = inner_width // mode_count
    free_cols = mid_width // contract_cols
    block_count = slice_ids.shape[1]
    first_all = jax.vmap(widen_first)(jnp.take(w1_table, mode_perm, axis=3))
    second_all = jax.vmap(widen_second)(w2_table)
    own_slices = slice_ids[0]
    begin = jnp.zeros((piece_rows, free_cols, 2 * out_width), jnp.float32)

    def one_block(block_index, running):
        stem_part = broadcast(stem_blocks[0], "cuts", block_index)
        slice_pair = own_slices[block_index]
        weight_one = lax.dynamic_index_in_dim(first_all, slice_pair[0], 0, keepdims=False)
        product = jnp.dot(
            stem_part.reshape(row_count, 2 * stem_width),
            weight_one,
            preferred_element_type=jnp.float32,
        ).astype(jnp.bfloat16)
        exchanged = lax.all_to_all(
            product[None, None], "mode", split_axis=2, concat_axis=1, tiled=True
        )
        weight_two = lax.dynamic_index_in_dim(second_all, slice_pair[1], 0, keepdims=True)
        return running + second_step(exchanged, weight_two, contract_cols, free_cols)

    amplitude = lax.fori_loop(0, block_count, one_block, begin)
    summed = lax.psum_scatter(amplitude, "cuts", scatter_dimension=1, tiled=True)
    return summed.reshape(piece_rows, summed.shape[1], 2, out_width)


def solution(mesh):
    placed = (P("cuts", "mode", None, None), P(), P(), P("cuts", None, None), P())
    return jax.shard_map(
        on_device,
        mesh=mesh,
        in_specs=placed,
        out_specs=P("mode", "cuts", None, None),
        check_vma=False,
    )
```

profile of v0, /device:TPU:0, one launch (start us, length us, event | category | flops | bytes accessed | tf_op | source)
XLA Modules:
  0.0 173.1 jit_solution(13787529332660151836)
XLA Ops:
  7.4 3.2 %slice_bitcast_fusion.2 = (bf16[8,256,256]{2,1,0:T(8,128)(2,1)}, bf16[8,256,256]{2,1,0:T(8,128)(2,1)}) fusion(bf16[8,2,256,256]{3,2,1,0:T(8,128)(2,1)} %param.9), kind=kLoop, calls=%fused_computation.19 | loop fusion | bytes 4194304 | tf_op jit(solution)/shard_map/vmap()/squeeze | solution.py:20
  10.6 1.1 fusion.6
  11.7 0.9 copy-done.6
  12.6 3.1 %copy.29 = bf16[8,2,256,256]{2,0,3,1:T(8,128)(2,1)} copy(bf16[8,2,256,256]{3,2,1,0:T(8,128)(2,1)S(1)} %copy-done.6) | data formatting | bytes 4194304 | tf_op args[1]
  15.7 2.4 %gather_fusion = bf16[256,8,2,256]{3,1,2,0:T(8,128)(2,1)S(1)} fusion(bf16[8,2,256,256]{2,0,3,1:T(8,128)(2,1)} %copy.29, s32[1024]{0:T(1024)S(1)} %pad_clamp_fusion), kind=kCustom, calls=%fused_computation | custom fusion | bytes 4195328 | tf_op jit(solution)/shard_map/jit(_take)/gather | solution.py:45
  18.1 0.9 select_bitcast_fusion
  19.0 1.1 slice_bitcast_fusion
  20.2 13.0 %maximum_maximum_fusion = bf16[8,512,512]{1,0,2:T(8,128)(2,1)} fusion(bf16[8,256,256]{1,0,2:T(8,128)(2,1)} %get-tuple-element.171, bf16[8,256,256]{1,0,2:T(8,128)(2,1)S(1)} %fusion.7, bf16[8,256,256]{1,0,2:T(8,128)(2,1)S(1)} %get-tuple-element.170), kind=kLoop, calls=%fused_computation.12 | loop fusion | flops 16777216 | bytes 7340032 | tf_op jit(solution)/shard_map/vmap()/concatenate | solution.py:16
  33.3 7.7 %copy.34 = bf16[8,512,512]{2,1,0:T(8,128)(2,1)} copy(bf16[8,512,512]{1,0,2:T(8,128)(2,1)} %maximum_maximum_fusion) | data formatting | bytes 8388608
  41.0 1.9 %maximum_bitcast_fusion.1 = (bf16[1,8,256,512]{3,2,0,1:T(8,128)(2,1)S(1)}, bf16[1,8,256,512]{3,2,0,1:T(8,128)(2,1)S(1)}) fusion(bf16[8,256,256]{2,1,0:T(8,128)(2,1)S(1)} %copy-done.5, bf16[8,256,256]{2,1,0:T(8,128)(2,1)} %get-tuple-element.169, bf16[8,256,256]{2,1,0:T(8,128)(2,1)S(1)} %copy-done.4), kind=kLoop, calls=%fused_computation.14 | loop fusion | flops 8388608 | bytes 7340032 | tf_op jit(solution)/shard_map/vmap()/stack | solution.py:23
  42.9 2.3 %maximum_bitcast_fusion = bf16[8,2,256,512]{3,2,1,0:T(8,128)(2,1)} fusion(bf16[1,8,256,512]{3,2,0,1:T(8,128)(2,1)S(1)} %get-tuple-element.173, bf16[1,8,256,512]{3,2,0,1:T(8,128)(2,1)S(1)} %get-tuple-element.172), kind=kLoop, calls=%fused_computation.13 | loop fusion | flops 2097152 | bytes 8388608 | tf_op jit(solution)/shard_map/vmap()/transpose | solution.py:46
  45.3 104.0 %while.14 = (s32[]{:T(128)}, f32[16,16,512]{2,1,0:T(8,128)S(1)}, bf16[1,256,2,256]{3,2,1,0:T(2,128)(2,1)S(1)}, s32[2,2]{1,0:T(2,128)S(1)}, bf16[8,512,512]{2,1,0...) while((s32[]{:T(128)}, f32[16,16,512]{2,1,0:T(8,128)S(1)}, ...), condition=%wide.region_2.3_spmd.clone, body=%wide.region_0.0_spmd.clone.sunk | while | flops 269090816 | bytes 11534731 | solution.py:65
  48.9 25.5 %all-reduce.2.cloned.1.call-done = bf16[256,512]{1,0:T(8,128)(2,1)} async-done(((bf16[256,512]{1,0:T(8,128)(2,1)}), bf16[256,512]{1,0:T(8,128)(2,1)}) %all-reduce.2.cloned.1.call-update) | async-done | bytes 262160 | tf_op jit(solution)/shard_map/while/body/eval_jaxpr/psum | solution.py:9
  74.4 1.4 fusion.23
  76.7 2.2 %reduce.6 = bf16[256,512]{1,0:T(8,128)(2,1)S(1)} reduce(bf16[256,1,1,512]{3,2,1,0:T(2,128)(2,1)S(1)} %bitcast.79, bf16[]{:T(256)} %broadcast.40), dimensions={1,2}, to_apply=%bitcast.54.reduce_sub_computation | reduce | bytes 524290 | tf_op jit(solution)/shard_map/while
  79.0 0.9 reshape.66
  79.8 5.6 %all-to-all-start = ((bf16[16,2,4096]{2,1,0:T(2,128)(2,1)}), bf16[16,2,4096]{2,1,0:T(2,128)(2,1)S(1)}, u32[]{:S(2)}, u32[]{:S(2)}) async-start(bf16[16,2,4096]{2,1,0:T(2,128)(2,1)} %reshape.66), calls=%async_computation | async-start | bytes 524288 | tf_op jit(solution)/shard_map/while/body/eval_jaxpr/all_to_all | solution.py:59
  87.5 1.1 constant_dynamic-slice_fusion.5
  88.6 6.9 %all-to-all-done = bf16[16,2,4096]{2,1,0:T(2,128)(2,1)S(1)} async-done(((bf16[16,2,4096]{2,1,0:T(2,128)(2,1)}), bf16[16,2,4096]{2,1,0:T(2,128)(2,1)S(1)}, u32[]{:S(2)}, u32[]{:S(2)}) %all-to-all-start) | async-done | bytes 262176 | tf_op jit(solution)/shard_map/while/body/eval_jaxpr/all_to_all | solution.py:59
  95.8 1.5 bitcast_reduce_fusion.2
  97.3 1.7 reshape.68
  103.5 20.2 %all-reduce.2.cloned.1.call-done = bf16[256,512]{1,0:T(8,128)(2,1)} async-done(((bf16[256,512]{1,0:T(8,128)(2,1)}), bf16[256,512]{1,0:T(8,128)(2,1)}) %all-reduce.2.cloned.1.call-update) | async-done | bytes 262160 | tf_op jit(solution)/shard_map/while/body/eval_jaxpr/psum | solution.py:9
  123.7 1.4 fusion.23
  126.1 2.2 %reduce.6 = bf16[256,512]{1,0:T(8,128)(2,1)S(1)} reduce(bf16[256,1,1,512]{3,2,1,0:T(2,128)(2,1)S(1)} %bitcast.79, bf16[]{:T(256)} %broadcast.40), dimensions={1,2}, to_apply=%bitcast.54.reduce_sub_computation | reduce | bytes 524290 | tf_op jit(solution)/shard_map/while
  128.3 0.9 reshape.66
  129.2 5.6 %all-to-all-start = ((bf16[16,2,4096]{2,1,0:T(2,128)(2,1)}), bf16[16,2,4096]{2,1,0:T(2,128)(2,1)S(1)}, u32[]{:S(2)}, u32[]{:S(2)}) async-start(bf16[16,2,4096]{2,1,0:T(2,128)(2,1)} %reshape.66), calls=%async_computation | async-start | bytes 524288 | tf_op jit(solution)/shard_map/while/body/eval_jaxpr/all_to_all | solution.py:59
  136.9 1.1 constant_dynamic-slice_fusion.5
  138.0 6.9 %all-to-all-done = bf16[16,2,4096]{2,1,0:T(2,128)(2,1)S(1)} async-done(((bf16[16,2,4096]{2,1,0:T(2,128)(2,1)}), bf16[16,2,4096]{2,1,0:T(2,128)(2,1)S(1)}, u32[]{:S(2)}, u32[]{:S(2)}) %all-to-all-start) | async-done | bytes 262176 | tf_op jit(solution)/shard_map/while/body/eval_jaxpr/all_to_all | solution.py:59
  145.1 1.5 bitcast_reduce_fusion.2
  146.6 1.7 reshape.68
  150.1 13.7 %reduce-scatter.2.cloned.1.call-done = f32[16,8,512]{2,1,0:T(8,128)} async-done(((f32[16,16,512]{2,1,0:T(8,128)}), f32[16,8,512]{2,1,0:T(8,128)}) %reduce-scatter.2.cloned.1.call-update) | async-done | bytes 262160 | tf_op jit(solution)/shard_map/reduce_scatter | solution.py:66
  163.8 1.8 %reshape.44 = f32[16,8,2,256]{3,2,1,0:T(2,128)} reshape(f32[16,8,512]{2,1,0:T(8,128)} %reduce-scatter.2.cloned.1.call-done) | data formatting | bytes 524288 | tf_op jit(solution)/shard_map/reshape | solution.py:67
  (46 shorter events, 8.5 us)
Async XLA Ops:
  7.4 3.2 %copy-start.3 = (bf16[8,2,256,256]{3,2,1,0:T(8,128)(2,1)S(1)}, bf16[8,2,256,256]{3,2,1,0:T(8,128)(2,1)}, u32[]{:S(2)}) copy-start(bf16[8,2,256,256]{3,2,1,0:T(8,128)(2,1)} %param.9) | copy-start | bytes 6291460
  7.4 4.3 %copy-start.7 = (s32[256]{0:T(256)S(1)}, s32[256]{0:T(256)}, u32[]{:S(2)}) copy-start(s32[256]{0:T(256)} %param.11) | copy-start | bytes 3076
  10.6 2.0 %copy-start.6 = (bf16[8,2,256,256]{3,2,1,0:T(8,128)(2,1)S(1)}, bf16[8,2,256,256]{3,2,1,0:T(8,128)(2,1)}, u32[]{:S(2)}) copy-start(bf16[8,2,256,256]{3,2,1,0:T(8,128)(2,1)} %param.8) | copy-start | bytes 6291460
  33.3 7.7 %copy-start.4 = (bf16[8,256,256]{2,1,0:T(8,128)(2,1)S(1)}, bf16[8,256,256]{2,1,0:T(8,128)(2,1)}, u32[]{:S(2)}) copy-start(bf16[8,256,256]{2,1,0:T(8,128)(2,1)} %fusion.6) | copy-start | bytes 3145732
  33.3 7.7 %copy-start.5 = (bf16[8,256,256]{2,1,0:T(8,128)(2,1)S(1)}, bf16[8,256,256]{2,1,0:T(8,128)(2,1)}, u32[]{:S(2)}) copy-start(bf16[8,256,256]{2,1,0:T(8,128)(2,1)} %get-tuple-element.168) | copy-start | bytes 3145732
  42.9 2.4 %copy-start.1 = (bf16[1,256,2,256]{3,2,1,0:T(2,128)(2,1)S(1)}, bf16[1,256,2,256]{3,2,1,0:T(2,128)(2,1)}, u32[]{:S(2)}) copy-start(bf16[1,256,2,256]{3,2,1,0:T(2,128)(2,1)} %param.7) | copy-start | bytes 786436
  42.9 2.4 %copy-start.8 = (s32[1,2,2]{2,1,0:T(2,128)S(1)}, s32[1,2,2]{2,1,0:T(2,128)}, u32[]{:S(2)}) copy-start(s32[1,2,2]{2,1,0:T(2,128)} %param.10) | copy-start | bytes 52
  45.3 29.1 %all-reduce.2.cloned.1.call-start = ((), (), s32[]{:S(2)}) async-start(), calls=%async_computation.3 | async-start | bytes 524288 | tf_op jit(solution)/shard_map/while/body/eval_jaxpr/psum | solution.py:9
  79.8 15.7 %all-to-all-start = ((bf16[16,2,4096]{2,1,0:T(2,128)(2,1)}), bf16[16,2,4096]{2,1,0:T(2,128)(2,1)S(1)}, u32[]{:S(2)}, u32[]{:S(2)}) async-start(bf16[16,2,4096]{2,1,0:T(2,128)(2,1)} %reshape.66), calls=%async_computation | async-start | bytes 524288 | tf_op jit(solution)/shard_map/while/body/eval_jaxpr/all_to_all | solution.py:59
  99.0 1.0 copy-start.2
  99.9 23.8 %all-reduce.2.cloned.1.call-start = ((), (), s32[]{:S(2)}) async-start(), calls=%async_computation.3 | async-start | bytes 524288 | tf_op jit(solution)/shard_map/while/body/eval_jaxpr/psum | solution.py:9
  129.2 15.7 %all-to-all-start = ((bf16[16,2,4096]{2,1,0:T(2,128)(2,1)}), bf16[16,2,4096]{2,1,0:T(2,128)(2,1)S(1)}, u32[]{:S(2)}, u32[]{:S(2)}) async-start(bf16[16,2,4096]{2,1,0:T(2,128)(2,1)} %reshape.66), calls=%async_computation | async-start | bytes 524288 | tf_op jit(solution)/shard_map/while/body/eval_jaxpr/all_to_all | solution.py:59
  148.3 1.0 copy-start.2
  149.3 0.8 copy-start
  149.3 14.5 %reduce-scatter.2.cloned.1.call-start = ((), (), s32[]{:S(2)}) async-start(), calls=%async_computation.2 | async-start | bytes 786432 | tf_op jit(solution)/shard_map/reduce_scatter | solution.py:66
Sparse Core Ops, SparseCore 0:
  48.5 25.8 all-reduce.1
  103.1 20.5 all-reduce.1
Sparse Core Ops, SparseCore 1:
  152.0 11.8 reduce-scatter.1
where the time goes:
time: 174 us; the launch traced here: 173 us
  waiting for transfers between devices  73.3 us (42%)
  local copies, waits for them, and re-layouts  37 us (21%)
  other arithmetic  24.2 us (14%)
  between operations  14.9 us (9%)
  starting transfers between devices  11.3 us (6%)
  loops' own time  8.19 us (5%)
  matrix products  4.28 us (2%)
    psum x2, waiting for transfers between devices, broadcast(): return lax.psum(block, axis)  45.7 us
    all_to_all x2, waiting for transfers between devices, one_block(): lax.all_to_all(product[None, None], 'mode', split_axis=2, concat_axis=1,...  13.8 us
    reduce_scatter x1, waiting for transfers between devices, on_device(): lax.psum_scatter(amplitude, 'cuts', scatter_dimension=1, tiled=True)  13.7 us
    concatenate x1, other arithmetic, widen_first(): return jnp.concatenate([upper, lower], axis=0)  13 us
    unnamed x18, local copies, waits for them, and re-layouts  12.5 us
    all_to_all x2, starting transfers between devices, one_block(): lax.all_to_all(product[None, None], 'mode', split_axis=2, concat_axis=1,...  11.2 us
    another operation x1, loops' own time, on_device(): amplitude = lax.fori_loop(0, block_count, one_block, begin)  8.19 us
    while x12, local copies, waits for them, and re-layouts  5.23 us
  transfers between devices with their start and end apart: 5, of which 5 were waited for; matrix products, arithmetic and copies ran while one was open for 2% of the time, Pallas kernels for 0%

commit v1 on v0

--- a/solution.py
+++ b/solution.py
@@ -6,7 +6,7 @@
 
 def broadcast(block, axis, source):
     block = jnp.where(lax.axis_index(axis) == source, block, jnp.zeros_like(block))
-    return lax.psum(block, axis)
+    return jnp.sum(lax.all_gather(block, axis), axis=0)
 
 
 def widen_first(entry):

time: 174 us -> 143 us (0.82)
  waiting for transfers between devices: 73.3 us -> 27.1 us
  blocking collectives: 0 us -> 18.7 us
    psum x2 -> x0, waiting for transfers between devices: 45.7 us -> none  [broadcast(): return lax.psum(block, axis)]
    all_gather x0 -> x2, blocking collectives: none -> 18.7 us  [broadcast(): return jnp.sum(lax.all_gather(block, axis), axis=0)]
    while x12 -> x14, local copies, waits for them, and re-layouts: 5.23 us -> 3.77 us
    unnamed x18 -> x17, local copies, waits for them, and re-layouts: 12.5 us -> 13.1 us
  transfers between devices with their start and end apart: 5 -> 3, of which waited for: 5 -> 3; matrix products, arithmetic and copies ran while one was open for 2% -> 2% of each run, Pallas kernels for 0% -> 0%
where the time goes in v1:
time: 143 us; the launch traced here: 142 us
  local copies, waits for them, and re-layouts  36.3 us (25%)
  waiting for transfers between devices  27.1 us (19%)
  other arithmetic  24.2 us (17%)
  blocking collectives  18.7 us (13%)
  between operations  13.5 us (9%)
  starting transfers between devices  9.74 us (7%)
  loops' own time  7.92 us (6%)
  matrix products  4.17 us (3%)
    all_gather x2, blocking collectives, broadcast(): return jnp.sum(lax.all_gather(block, axis), axis=0)  18.7 us
    all_to_all x2, waiting for transfers between devices, one_block(): lax.all_to_all(product[None, None], 'mode', split_axis=2, concat_axis=1,...  14.1 us
    unnamed x17, local copies, waits for them, and re-layouts  13.1 us
    concatenate x1, other arithmetic, widen_first(): return jnp.concatenate([upper, lower], axis=0)  13.1 us
    reduce_scatter x1, waiting for transfers between devices, on_device(): lax.psum_scatter(amplitude, 'cuts', scatter_dimension=1, tiled=True)  13 us
    all_to_all x2, starting transfers between devices, one_block(): lax.all_to_all(product[None, None], 'mode', split_axis=2, concat_axis=1,...  9.73 us
    another operation x1, loops' own time, on_device(): amplitude = lax.fori_loop(0, block_count, one_block, begin)  7.92 us
    while x2, other arithmetic  4.41 us
  transfers between devices with their start and end apart: 3, of which 3 were waited for; matrix products, arithmetic and copies ran while one was open for 2% of the time, Pallas kernels for 0%

profile of v1, /device:TPU:0, one launch (start us, length us, event | category | flops | bytes accessed | tf_op | source)
XLA Modules:
  0.0 141.5 jit_solution(9377215386235271836)
XLA Ops:
  6.5 3.2 %slice_bitcast_fusion.2 = (bf16[8,256,256]{2,1,0:T(8,128)(2,1)}, bf16[8,256,256]{2,1,0:T(8,128)(2,1)}) fusion(bf16[8,2,256,256]{3,2,1,0:T(8,128)(2,1)} %param.9), kind=kLoop, calls=%fused_computation.19 | loop fusion | bytes 4194304 | tf_op jit(solution)/shard_map/vmap()/squeeze | solution.py:20
  9.8 1.1 fusion.6
  10.8 4.5 %copy.51 = bf16[8,2,256,256]{2,0,3,1:T(8,128)(2,1)} copy(bf16[8,2,256,256]{3,2,1,0:T(8,128)(2,1)} %param.8) | data formatting | bytes 4194304 | tf_op args[1]
  15.4 2.4 %gather_fusion = bf16[256,8,2,256]{3,1,2,0:T(8,128)(2,1)S(1)} fusion(bf16[8,2,256,256]{2,0,3,1:T(8,128)(2,1)} %copy.51, s32[1024]{0:T(1024)S(1)} %pad_clamp_fusion), kind=kCustom, calls=%fused_computation | custom fusion | bytes 4195328 | tf_op jit(solution)/shard_map/jit(_take)/gather | solution.py:45
  17.8 0.9 select_bitcast_fusion
  18.7 1.1 slice_bitcast_fusion
  19.9 13.1 %maximum_maximum_fusion = bf16[8,512,512]{1,0,2:T(8,128)(2,1)} fusion(bf16[8,256,256]{1,0,2:T(8,128)(2,1)} %get-tuple-element.228, bf16[8,256,256]{1,0,2:T(8,128)(2,1)S(1)} %fusion.7, bf16[8,256,256]{1,0,2:T(8,128)(2,1)S(1)} %get-tuple-element.227), kind=kLoop, calls=%fused_computation.12 | loop fusion | flops 16777216 | bytes 7340032 | tf_op jit(solution)/shard_map/vmap()/concatenate | solution.py:16
  33.0 7.8 %copy.57 = bf16[8,512,512]{2,1,0:T(8,128)(2,1)} copy(bf16[8,512,512]{1,0,2:T(8,128)(2,1)} %maximum_maximum_fusion) | data formatting | bytes 8388608
  40.8 1.9 %maximum_bitcast_fusion.1 = (bf16[1,8,256,512]{3,2,0,1:T(8,128)(2,1)S(1)}, bf16[1,8,256,512]{3,2,0,1:T(8,128)(2,1)S(1)}) fusion(bf16[8,256,256]{2,1,0:T(8,128)(2,1)S(1)} %copy-done.5, bf16[8,256,256]{2,1,0:T(8,128)(2,1)} %get-tuple-element.226, bf16[8,256,256]{2,1,0:T(8,128)(2,1)S(1)} %copy-done.4), kind=kLoop, calls=%fused_computation.14 | loop fusion | flops 8388608 | bytes 7340032 | tf_op jit(solution)/shard_map/vmap()/stack | solution.py:23
  42.7 2.3 %maximum_bitcast_fusion = bf16[8,2,256,512]{3,2,1,0:T(8,128)(2,1)} fusion(bf16[1,8,256,512]{3,2,0,1:T(8,128)(2,1)S(1)} %get-tuple-element.230, bf16[1,8,256,512]{3,2,0,1:T(8,128)(2,1)S(1)} %get-tuple-element.229), kind=kLoop, calls=%fused_computation.13 | loop fusion | flops 2097152 | bytes 8388608 | tf_op jit(solution)/shard_map/vmap()/transpose | solution.py:46
  45.1 74.0 %while.16 = (s32[]{:T(128)}, f32[16,16,512]{2,1,0:T(8,128)S(1)}, bf16[1,256,2,256]{3,1,2,0:T(8,128)(2,1)S(1)}, s32[2,2]{1,0:T(2,128)S(1)}, bf16[8,512,512]{2,1,0...) while((s32[]{:T(128)}, f32[16,16,512]{2,1,0:T(8,128)S(1)}, ...), condition=%wide.region_2.3_spmd.clone, body=%wide.region_0.0_spmd.clone.sunk | while | flops 269090816 | bytes 12583297 | solution.py:65
  47.0 9.9 %all_gather.15 = bf16[2,256,2,256]{3,1,2,0:T(8,128)(2,1)S(1)} all-gather(bf16[1,256,2,256]{3,1,2,0:T(8,128)(2,1)S(1)} %broadcast_select_fusion.2), channel_id=1, replica_groups=mesh['cuts'=2,'mode'=16] {'cuts'}, dimensions={0}, use_global_device_ids=true | all-gather | bytes 786432 | tf_op jit(solution)/shard_map/while/body/eval_jaxpr/all_gather | solution.py:9
  57.9 1.4 fusion.23
  60.2 2.2 %reduce.12 = bf16[256,512]{1,0:T(8,128)(2,1)S(1)} reduce(bf16[256,1,1,512]{3,2,1,0:T(2,128)(2,1)S(1)} %bitcast.75, bf16[]{:T(256)} %broadcast.58), dimensions={1,2}, to_apply=%bitcast.52.reduce_sub_computation | reduce | bytes 524290 | tf_op jit(solution)/shard_map/while
  62.4 0.9 reshape.77
  63.3 6.2 %all-to-all-start = ((bf16[16,2,4096]{2,1,0:T(2,128)(2,1)}), bf16[16,2,4096]{2,1,0:T(2,128)(2,1)S(1)}, u32[]{:S(2)}, u32[]{:S(2)}) async-start(bf16[16,2,4096]{2,1,0:T(2,128)(2,1)} %reshape.77), calls=%async_computation | async-start | bytes 524288 | tf_op jit(solution)/shard_map/while/body/eval_jaxpr/all_to_all | solution.py:59
  71.4 1.1 constant_dynamic-slice_fusion.5
  72.5 7.1 %all-to-all-done = bf16[16,2,4096]{2,1,0:T(2,128)(2,1)S(1)} async-done(((bf16[16,2,4096]{2,1,0:T(2,128)(2,1)}), bf16[16,2,4096]{2,1,0:T(2,128)(2,1)S(1)}, u32[]{:S(2)}, u32[]{:S(2)}) %all-to-all-start) | async-done | bytes 262176 | tf_op jit(solution)/shard_map/while/body/eval_jaxpr/all_to_all | solution.py:59
  79.9 1.5 %bitcast_reduce_fusion.2 = bf16[256,512]{1,0:T(8,128)(2,1)S(1)} fusion(bf16[256,1,1,512]{3,2,1,0:T(2,128)(2,1)S(1)} %reshape.78), kind=kLoop, calls=%fused_computation.27.clone.1 | loop fusion | bytes 524288 | tf_op jit(solution)/shard_map/while/body/eval_jaxpr/all_to_all | solution.py:59
  81.4 1.7 %reshape.79 = bf16[16,16,2,16,16]{4,3,2,1,0:T(8,128)(2,1)S(1)} reshape(bf16[256,512]{1,0:T(8,128)(2,1)S(1)} %bitcast_reduce_fusion.2) | data formatting | bytes 524288 | tf_op jit(solution)/shard_map/reshape.42
  86.0 8.7 %all_gather.15 = bf16[2,256,2,256]{3,1,2,0:T(8,128)(2,1)S(1)} all-gather(bf16[1,256,2,256]{3,1,2,0:T(8,128)(2,1)S(1)} %broadcast_select_fusion.2), channel_id=1, replica_groups=mesh['cuts'=2,'mode'=16] {'cuts'}, dimensions={0}, use_global_device_ids=true | all-gather | bytes 786432 | tf_op jit(solution)/shard_map/while/body/eval_jaxpr/all_gather | solution.py:9
  95.7 1.4 fusion.23
  98.0 2.2 %reduce.12 = bf16[256,512]{1,0:T(8,128)(2,1)S(1)} reduce(bf16[256,1,1,512]{3,2,1,0:T(2,128)(2,1)S(1)} %bitcast.75, bf16[]{:T(256)} %broadcast.58), dimensions={1,2}, to_apply=%bitcast.52.reduce_sub_computation | reduce | bytes 524290 | tf_op jit(solution)/shard_map/while
  100.2 0.9 reshape.77
  101.1 3.5 %all-to-all-start = ((bf16[16,2,4096]{2,1,0:T(2,128)(2,1)}), bf16[16,2,4096]{2,1,0:T(2,128)(2,1)S(1)}, u32[]{:S(2)}, u32[]{:S(2)}) async-start(bf16[16,2,4096]{2,1,0:T(2,128)(2,1)} %reshape.77), calls=%async_computation | async-start | bytes 524288 | tf_op jit(solution)/shard_map/while/body/eval_jaxpr/all_to_all | solution.py:59
  106.5 1.1 constant_dynamic-slice_fusion.5
  107.6 7.0 %all-to-all-done = bf16[16,2,4096]{2,1,0:T(2,128)(2,1)S(1)} async-done(((bf16[16,2,4096]{2,1,0:T(2,128)(2,1)}), bf16[16,2,4096]{2,1,0:T(2,128)(2,1)S(1)}, u32[]{:S(2)}, u32[]{:S(2)}) %all-to-all-start) | async-done | bytes 262176 | tf_op jit(solution)/shard_map/while/body/eval_jaxpr/all_to_all | solution.py:59
  114.9 1.5 %bitcast_reduce_fusion.2 = bf16[256,512]{1,0:T(8,128)(2,1)S(1)} fusion(bf16[256,1,1,512]{3,2,1,0:T(2,128)(2,1)S(1)} %reshape.78), kind=kLoop, calls=%fused_computation.27.clone.1 | loop fusion | bytes 524288 | tf_op jit(solution)/shard_map/while/body/eval_jaxpr/all_to_all | solution.py:59
  116.4 1.7 %reshape.79 = bf16[16,16,2,16,16]{4,3,2,1,0:T(8,128)(2,1)S(1)} reshape(bf16[256,512]{1,0:T(8,128)(2,1)S(1)} %bitcast_reduce_fusion.2) | data formatting | bytes 524288 | tf_op jit(solution)/shard_map/reshape.42
  119.1 0.8 copy-done
  119.9 13.0 %reduce-scatter.2.cloned.1.call-done = f32[16,8,512]{2,1,0:T(8,128)} async-done(((f32[16,16,512]{2,1,0:T(8,128)}), f32[16,8,512]{2,1,0:T(8,128)}) %reduce-scatter.2.cloned.1.call-update) | async-done | bytes 262160 | tf_op jit(solution)/shard_map/reduce_scatter | solution.py:66
  132.9 1.8 %reshape.56 = f32[16,8,2,256]{3,2,1,0:T(2,128)} reshape(f32[16,8,512]{2,1,0:T(8,128)} %reduce-scatter.2.cloned.1.call-done) | data formatting | bytes 524288 | tf_op jit(solution)/shard_map/reshape | solution.py:67
  (47 shorter events, 6.3 us)
Async XLA Ops:
  6.5 3.2 %copy-start.3 = (bf16[8,2,256,256]{3,2,1,0:T(8,128)(2,1)S(1)}, bf16[8,2,256,256]{3,2,1,0:T(8,128)(2,1)}, u32[]{:S(2)}) copy-start(bf16[8,2,256,256]{3,2,1,0:T(8,128)(2,1)} %param.9) | copy-start | bytes 6291460
  6.5 4.3 %copy-start.7 = (s32[256]{0:T(256)S(1)}, s32[256]{0:T(256)}, u32[]{:S(2)}) copy-start(s32[256]{0:T(256)} %param.11) | copy-start | bytes 3076
  6.5 126.3 %reduce-scatter.2.cloned.1.call-start = ((), (), s32[]{:S(2)}) async-start(), calls=%async_computation.2 | async-start | bytes 786432 | tf_op jit(solution)/shard_map/reduce_scatter | solution.py:66
  33.0 7.8 %copy-start.6 = (bf16[1,256,2,256]{3,2,1,0:T(2,128)(2,1)S(1)}, bf16[1,256,2,256]{3,2,1,0:T(2,128)(2,1)}, u32[]{:S(2)}) copy-start(bf16[1,256,2,256]{3,2,1,0:T(2,128)(2,1)} %param.7) | copy-start | bytes 786436
  33.0 7.8 %copy-start.4 = (bf16[8,256,256]{2,1,0:T(8,128)(2,1)S(1)}, bf16[8,256,256]{2,1,0:T(8,128)(2,1)}, u32[]{:S(2)}) copy-start(bf16[8,256,256]{2,1,0:T(8,128)(2,1)} %fusion.6) | copy-start | bytes 3145732
  33.0 7.8 %copy-start.5 = (bf16[8,256,256]{2,1,0:T(8,128)(2,1)S(1)}, bf16[8,256,256]{2,1,0:T(8,128)(2,1)}, u32[]{:S(2)}) copy-start(bf16[8,256,256]{2,1,0:T(8,128)(2,1)} %get-tuple-element.225) | copy-start | bytes 3145732
  42.7 2.4 %copy-start.8 = (s32[1,2,2]{2,1,0:T(2,128)S(1)}, s32[1,2,2]{2,1,0:T(2,128)}, u32[]{:S(2)}) copy-start(s32[1,2,2]{2,1,0:T(2,128)} %param.10) | copy-start | bytes 52
  45.1 1.9 %copy-start.1 = (bf16[1,256,2,256]{3,1,2,0:T(8,128)(2,1)}, bf16[1,256,2,256]{3,1,2,0:T(8,128)(2,1)S(1)}, u32[]{:S(2)}) copy-start(bf16[1,256,2,256]{3,1,2,0:T(8,128)(2,1)S(1)} %get-tuple-element.300) | copy-start | bytes 786436 | tf_op jit(solution)/shard_map/while
  63.3 16.3 %all-to-all-start = ((bf16[16,2,4096]{2,1,0:T(2,128)(2,1)}), bf16[16,2,4096]{2,1,0:T(2,128)(2,1)S(1)}, u32[]{:S(2)}, u32[]{:S(2)}) async-start(bf16[16,2,4096]{2,1,0:T(2,128)(2,1)} %reshape.77), calls=%async_computation | async-start | bytes 524288 | tf_op jit(solution)/shard_map/while/body/eval_jaxpr/all_to_all | solution.py:59
  83.1 1.0 copy-start.2
  84.0 1.9 %copy-start.1 = (bf16[1,256,2,256]{3,1,2,0:T(8,128)(2,1)}, bf16[1,256,2,256]{3,1,2,0:T(8,128)(2,1)S(1)}, u32[]{:S(2)}) copy-start(bf16[1,256,2,256]{3,1,2,0:T(8,128)(2,1)S(1)} %get-tuple-element.300) | copy-start | bytes 786436 | tf_op jit(solution)/shard_map/while
  101.1 13.5 %all-to-all-start = ((bf16[16,2,4096]{2,1,0:T(2,128)(2,1)}), bf16[16,2,4096]{2,1,0:T(2,128)(2,1)S(1)}, u32[]{:S(2)}, u32[]{:S(2)}) async-start(bf16[16,2,4096]{2,1,0:T(2,128)(2,1)} %reshape.77), calls=%async_computation | async-start | bytes 524288 | tf_op jit(solution)/shard_map/while/body/eval_jaxpr/all_to_all | solution.py:59
  118.1 1.0 copy-start.2
  119.1 0.8 copy-start
Sparse Core Ops, SparseCore 0:
  120.0 12.8 reduce-scatter.1
